TPU v7x, 256 devices: a whole 4x4x8 slice. The times are simulated.
256 devices in a mesh: row: 32 (over x, y, core), col: 8 (over z).
Axes of the slice: x: 4, y: 4, z: 8, core: 2. Of those that a mesh axis runs over, the one named last changes fastest.
Arguments:
- leaf_points: float32 [128, 8, 256], P('row'), may hold values from -6 to 6
- col_points: float32 [8, 512, 8, 256], P('col', 'row'), may hold values from -6 to 6
- source_hash_signs: int32 [8, 512, 256], P('col'), may hold values from 0 to 255
- adjacent_leaf_lists: int32 [128, 384], P('row', 'col'), may hold values from 0 to 511
- near_count: int32 [128, 8], P('row', 'col'), may hold values from 1 to 48, as said below
Outputs:
- leaf_basis: float32 [128, 256, 128], P('row', 'col')
- top_factor: float32 [32, 128, 128], P('row')
Inputs may be any that keep to these rules, and one draw needn't show every extreme that they name: `adjacent_leaf_lists`: A column leaf number local to owner c; slots at or beyond the pair's count are unused. `near_count`: some pair has exactly 48 used slots. `source_hash_signs`: the bucket is code % 128, the sign is negative where code >= 128.
All inputs are finite; a program needn't handle non-finite values.
Results may differ from a plain program's by a relative error of at most 0.0003.
Values sent between devices are 32-bit elements; how exact they have to be, the bound alone decides.
No kernel may reach another device: no remote copies, remote signals or barrier semaphores. Data moves between devices by JAX's collectives and lax.ppermute only.
A program may use at most 64 MiB of HBM per device.

v0:
```python
from functools import partial

import jax
import jax.numpy as jnp
from jax import lax
from jax.sharding import PartitionSpec as P
from jax.experimental import pallas as pl
from jax.experimental.pallas import tpu as pltpu

SK = 128
MERGED_LEVELS = 4


half_inverse = 0.125
ridge_eps = 1e-05


def from_partner(value, axis, stride):
    mask = 2**stride
    pairs = [(source, source ^ mask) for source in range(lax.axis_size(axis))]
    return lax.ppermute(value, axis, pairs)


def split3(value):
    first = value.astype(jnp.bfloat16)
    rest = value - first.astype(jnp.float32)
    second = rest.astype(jnp.bfloat16)
    third = (rest - second.astype(jnp.float32)).astype(jnp.bfloat16)
    return first, second, third


def row_operand(leaf_points):
    norms = jnp.sum(leaf_points * leaf_points, axis=1)
    scaled = jnp.swapaxes(leaf_points, 1, 2) * (2.0 * half_inverse)
    place = lax.broadcasted_iota(jnp.int32, norms.shape + (8,), 2)
    tail = jnp.where(place == 0, -half_inverse, jnp.where(place == 1, -half_inverse * norms[:, :, None], 0.0))
    first, second, third = split3(jnp.concatenate([scaled, tail], axis=2))
    return jnp.concatenate([first, first, second, second, first, third], axis=2)


def sketch_kernel(slots_ref, counts_ref, row_ref, col_ref, code_ref, out_ref):
    leaves = out_ref.shape[0]
    points = col_ref.shape[2]
    place = lax.broadcasted_iota(jnp.int32, (8, points), 0)
    bucket_id = lax.broadcasted_iota(jnp.int32, (SK, points), 0)
    contract_last = (((1,), (1,)), ((), ()))
    for leaf in range(leaves):
        out_ref[leaf] = jnp.zeros(out_ref.shape[1:], jnp.float32)

        def tile(slot, carry):
            column = slots_ref[leaf, slot]
            y = col_ref[column]
            norms = jnp.sum(y * y, axis=0, keepdims=True)
            tail = jnp.where(place == 0, norms, jnp.where(place == 1, 1.0, 0.0))
            first, second, third = split3(jnp.concatenate([y, tail], axis=0))
            stacked = jnp.concatenate([first, second, first, second, third, first], axis=0)
            exponent = jnp.dot(row_ref[leaf], stacked, preferred_element_type=jnp.float32)
            kernel = jnp.exp(exponent)
            code = code_ref[pl.ds(column, 1), :]
            signs = (1 - 2 * (code // SK)).astype(jnp.float32)
            omega_t = jnp.where(bucket_id == code % SK, signs, 0.0).astype(jnp.bfloat16)
            high = kernel.astype(jnp.bfloat16)
            low = (kernel - high.astype(jnp.float32)).astype(jnp.bfloat16)
            terms = lax.dot_general(high, omega_t, contract_last, preferred_element_type=jnp.float32)
            terms = terms + lax.dot_general(low, omega_t, contract_last, preferred_element_type=jnp.float32)
            out_ref[leaf] += terms
            return carry

        def two_tiles(step, carry):
            return tile(2 * step + 1, tile(2 * step, carry))

        count = counts_ref[leaf]
        lax.fori_loop(0, count // 2, two_tiles, 0)
        lax.fori_loop((count // 2) * 2, count, tile, 0)


def accumulate(leaf_points, col_store, code_store, slot_table, pair_count):
    leaves, _, points = leaf_points.shape
    smem, vmem = pltpu.MemorySpace.SMEM, pltpu.MemorySpace.VMEM
    return pl.pallas_call(
        sketch_kernel,
        out_shape=jax.ShapeDtypeStruct((leaves, points, SK), jnp.float32),
        in_specs=[pl.BlockSpec(memory_space=smem)] * 2 + [pl.BlockSpec(memory_space=vmem)] * 3,
        out_specs=pl.BlockSpec(memory_space=vmem),
        compiler_params=pltpu.CompilerParams(vmem_limit_bytes=48 * 1024 * 1024),
    )(slot_table, pair_count, row_operand(leaf_points), col_store, code_store)


def on_device(leaf_points, col_points, source_hash_signs, adjacent_leaf_lists, near_count):
    owned = lax.all_gather(col_points, "row", axis=1, tiled=True)
    leaves = leaf_points.shape[0]
    pair_count = near_count[:, 0]
    samples = accumulate(
        leaf_points,
        owned.reshape(owned.shape[1:]),
        source_hash_signs.reshape(source_hash_signs.shape[1:]),
        adjacent_leaf_lists,
        pair_count,
    )
    samples = lax.psum(samples, "col")
    rows = samples.shape[1] // lax.axis_size("col")
    rows_part = lax.dynamic_slice_in_dim(samples, lax.axis_index("col") * rows, rows, axis=1)
    gram = jnp.einsum("bri,brk->bik", samples, samples, precision=lax.Precision.HIGHEST)
    ridge = jnp.trace(gram, axis1=1, axis2=2) / SK + ridge_eps
    shifted = gram + ridge[:, None, None] * jnp.eye(SK, dtype=jnp.float32)[None]
    lower = jnp.linalg.cholesky(shifted)
    triangular_backsubstitute = jax.vmap(partial(jax.scipy.linalg.solve_triangular, lower=True))
    leaf_basis = jnp.swapaxes(triangular_backsubstitute(lower, jnp.swapaxes(rows_part, 1, 2)), 1, 2)
    total = jnp.sum(shifted, axis=0)
    local_levels = leaves.bit_length() - 1
    for bit in range(MERGED_LEVELS - local_levels):
        total = total + from_partner(total, "row", bit)
    factor = jnp.swapaxes(jnp.linalg.cholesky(total[None]), 1, 2)
    return (leaf_basis, factor)


def solution(mesh):
    return jax.shard_map(
        on_device,
        mesh=mesh,
        in_specs=(
            P("row", None, None),
            P("col", "row", None, None),
            P("col", None, None),
            P("row", "col"),
            P("row", "col"),
        ),
        out_specs=(P("row", "col", None), P("row", None, None)),
        check_vma=False,
    )
```

profile of v0, /device:TPU:22, one launch (start us, length us, event | category | flops | bytes accessed | tf_op | source)
XLA Modules:
  0.0 306.5 jit_solution(14309332960940066469)
XLA Ops:
  7.2 0.7 all-gather.2.cloned.1.call-update
  8.0 0.8 multiply_bitcast_fusion
  8.9 0.1 copy.35
  9.0 0.2 copy.36
  9.2 0.2 copy.34
  9.5 0.7 concatenate.7.row_ref
  10.2 52.3 %all-gather.2.cloned.1.call-done = f32[1,512,8,256]{3,2,0,1:T(8,128)} async-done(((f32[1,16,8,256]{3,2,0,1:T(8,128)}), f32[1,512,8,256]{3,2,0,1:T(8,128)}) %all-gather.2.cloned.1.call-update) | async-done | bytes 4194320 | tf_op jit(solution)/shard_map/all_gather | solution.py:90
  62.5 2.2 copy-done
  64.7 19.6 %shard_map.68 = f32[4,256,128]{2,1,0:T(8,128)} custom-call(s32[4,48]{1,0:T(4,128)S(1)} %copy-done.2, s32[4]{0:T(128)S(1)} %bitcast.30, bf16[4,256,96]{2,1,0:T(8,128)(2,1)S(1)} %concatenate.7.row_ref, f32[512,8,256]{2,1,0:T(8,128)S(1)} %bitcast.28, s32[512,256]{1,0:T(8,128)S(1)} %bitcast.29), custom_call_target="tpu_custom_call" | custom-call | tf_op jit(solution)/shard_map/pallas_call | solution.py:80
  84.4 107.3 %all-reduce.2.cloned.1.call-done = f32[4,256,128]{2,1,0:T(8,128)} async-done(((f32[4,256,128]{2,1,0:T(8,128)}), f32[4,256,128]{2,1,0:T(8,128)}) %all-reduce.2.cloned.1.call-update) | async-done | bytes 524304 | tf_op jit(solution)/shard_map/psum | solution.py:100
  191.7 2.3 select_reduce_fusion.1
  194.0 0.1 copy.41
  194.2 0.1 fusion.4
  194.5 46.9 %custom-call.12 = f32[4,128,128]{2,1,0:T(8,128)S(1)} custom-call(f32[4,128,128]{2,1,0:T(8,128)S(1)} %get-tuple-element.13), custom_call_target="Cholesky" | custom-call | tf_op jit(solution)/shard_map/jit(cholesky)/cholesky | solution.py:106
  241.5 0.1 compare_reduce_fusion.1
  241.6 0.1 select_bitcast_fusion
  241.7 39.3 %custom-call.13 = f32[4,1,128,128]{2,3,1,0:T(8,128)S(1)} custom-call(f32[4,1,128,128]{3,2,1,0:T(8,128)S(1)} %select_bitcast_fusion), custom_call_target="InvertDiagBlocksLowerTriangular" | custom-call | tf_op jit(solution)/shard_map/vmap(jit(_solve_triangular))/triangular_solve | solution.py:108
  281.0 1.5 collective-permute-start.1
  282.5 1.8 fusion
  284.3 1.5 collective-permute-done.1
  285.9 11.7 %custom-call.14 = f32[1,128,128]{2,1,0:T(8,128)S(1)} custom-call(f32[1,128,128]{2,1,0:T(8,128)S(1)} %fusion.5), custom_call_target="Cholesky" | custom-call | tf_op jit(solution)/shard_map/jit(cholesky)/cholesky | solution.py:113
  297.7 0.6 compare_reduce_fusion
  298.3 0.7 select_bitcast_fusion.1
  299.0 0.7 copy.46
  (29 shorter events, 0.7 us)
Async XLA Ops:
  7.2 55.4 %copy-start.3 = (s32[4,1]{0,1:T(1,128)S(1)}, s32[4,1]{0,1:T(1,128)}, u32[]{:S(2)}) copy-start(s32[4,1]{0,1:T(1,128)} %param.9) | copy-start | bytes 52
  7.2 55.3 %copy-start.1 = (s32[1,512,256]{2,1,0:T(8,128)S(1)}, s32[1,512,256]{2,1,0:T(8,128)}, u32[]{:S(2)}) copy-start(s32[1,512,256]{2,1,0:T(8,128)} %param.7) | copy-start | bytes 1572868
  7.2 55.3 %copy-start.2 = (s32[4,48]{1,0:T(4,128)S(1)}, s32[4,48]{1,0:T(4,128)}, u32[]{:S(2)}) copy-start(s32[4,48]{1,0:T(4,128)} %slots_ref.1) | copy-start | bytes 2308
  7.2 55.3 %all-gather.2.cloned.1.call-start = ((), (), s32[]{:S(2)}) async-start(), calls=%async_computation | async-start | bytes 4325376 | tf_op jit(solution)/shard_map/all_gather | solution.py:90
  7.9 183.8 %all-reduce.2.cloned.1.call-start = ((), (), s32[]{:S(2)}) async-start(), calls=%async_computation.1 | async-start | bytes 1048576 | tf_op jit(solution)/shard_map/psum | solution.py:100
  62.5 2.2 copy-start
  194.4 86.6 %collective-permute-start = (f32[128,128]{0,1:T(8,128)S(1)}, f32[128,128]{0,1:T(8,128)S(1)}, u32[]{:S(2)}, u32[]{:S(2)}) collective-permute-start(f32[128,128]{0,1:T(8,128)S(1)} %copy.44), channel_id=1, source_target_pairs={{0,8},{8,0},{16,24},{24,16},{32,40},{40,32},{48,56},{56,48},{64,72... | collective-permute-start | bytes 196616 | tf_op jit(solution)/shard_map/ppermute | solution.py:21
  281.0 4.7 %collective-permute-start.1 = (f32[128,128]{0,1:T(8,128)S(1)}, f32[128,128]{0,1:T(8,128)S(1)}, u32[]{:S(2)}, u32[]{:S(2)}) collective-permute-start(f32[128,128]{0,1:T(8,128)S(1)} %add.50), channel_id=1, source_target_pairs={{0,16},{8,24},{16,0},{24,8},{32,48},{40,56},{48,32},{56,40},{64,80... | collective-permute-start | bytes 196616 | tf_op jit(solution)/shard_map/ppermute | solution.py:21
Sparse Core Ops, SparseCore 0:
  10.6 51.9 all-gather.1
  84.5 107.2 all-reduce.1
where the time goes:
time: 309 us; the launch traced here: 307 us
  waiting for transfers between devices  162 us (52%)
  other arithmetic  101 us (33%)
  Pallas kernels  19.6 us (6%)
  between operations  14.2 us (5%)
  local copies, waits for them, and re-layouts  4.46 us (1%)
  matrix products  4.09 us (1%)
    psum x1, waiting for transfers between devices, on_device(): samples = lax.psum(samples, 'col')  107 us
    all_gather x1, waiting for transfers between devices, on_device(): owned = lax.all_gather(col_points, 'row', axis=1, tiled=True)  52.3 us
    another operation x4, other arithmetic, on_device(): lower = jnp.linalg.cholesky(shifted)  47.1 us
    another operation x3, other arithmetic, on_device(): triangular_backsubstitute(lower, jnp.swapaxes(rows_part, 1, 2))  39.4 us
    pallas_call x1, Pallas kernels, accumulate(): pl.pallas_call(sketch_kernel, out_shape=jax.ShapeDtypeStruct((leaves, poi...  19.6 us
    another operation x3, other arithmetic, on_device(): factor = jnp.swapaxes(jnp.linalg.cholesky(total[None]), 1, 2)  12.4 us
  transfers between devices with their start and end apart: 4, of which 3 were waited for; matrix products, arithmetic and copies ran while one was open for 30% of the time, Pallas kernels for 0%

commit v1 on v0

--- a/solution.py
+++ b/solution.py
@@ -86,6 +86,46 @@
     )(slot_table, pair_count, row_operand(leaf_points), col_store, code_store)
 
 
+def cholesky_kernel(in_ref, out_ref):
+    mats, rows, width = in_ref.shape
+    out_ref[...] = in_ref[...]
+    for block in range(width // 8):
+        low = block * 8
+        shape = (rows - low, width)
+        lane = lax.broadcasted_iota(jnp.int32, shape, 1)
+        row = lax.broadcasted_iota(jnp.int32, shape, 0) + low
+        parts = [out_ref[m, low:, :] for m in range(mats)]
+        for t in range(8):
+            j = low + t
+            pick = lane == j
+            later = lane > j
+            for m in range(mats):
+                a = parts[m]
+                pivot_row = a[t : t + 1]
+                pivot = jnp.sum(jnp.where(pick[:1], pivot_row, 0.0), axis=1, keepdims=True)
+                scale = 1.0 / jnp.sqrt(pivot)
+                column = jnp.sum(jnp.where(pick, a, 0.0), axis=1, keepdims=True) * scale
+                column = jnp.where(row[:, :1] >= j, column, 0.0)
+                updated = a - column * (pivot_row * scale)
+                parts[m] = jnp.where(later, updated, jnp.where(pick, column, a))
+        for m in range(mats):
+            out_ref[m, low:, :] = parts[m]
+    lane = lax.broadcasted_iota(jnp.int32, (rows, width), 1)
+    row = lax.broadcasted_iota(jnp.int32, (rows, width), 0)
+    for m in range(mats):
+        out_ref[m] = jnp.where(row >= lane, out_ref[m], 0.0)
+
+
+def cholesky_rows(stacked):
+    vmem = pltpu.MemorySpace.VMEM
+    return pl.pallas_call(
+        cholesky_kernel,
+        out_shape=jax.ShapeDtypeStruct(stacked.shape, jnp.float32),
+        in_specs=[pl.BlockSpec(memory_space=vmem)],
+        out_specs=pl.BlockSpec(memory_space=vmem),
+    )(stacked)
+
+
 def on_device(leaf_points, col_points, source_hash_signs, adjacent_leaf_lists, near_count):
     owned = lax.all_gather(col_points, "row", axis=1, tiled=True)
     leaves = leaf_points.shape[0]
@@ -103,14 +143,20 @@
     gram = jnp.einsum("bri,brk->bik", samples, samples, precision=lax.Precision.HIGHEST)
     ridge = jnp.trace(gram, axis1=1, axis2=2) / SK + ridge_eps
     shifted = gram + ridge[:, None, None] * jnp.eye(SK, dtype=jnp.float32)[None]
-    lower = jnp.linalg.cholesky(shifted)
-    triangular_backsubstitute = jax.vmap(partial(jax.scipy.linalg.solve_triangular, lower=True))
-    leaf_basis = jnp.swapaxes(triangular_backsubstitute(lower, jnp.swapaxes(rows_part, 1, 2)), 1, 2)
     total = jnp.sum(shifted, axis=0)
     local_levels = leaves.bit_length() - 1
     for bit in range(MERGED_LEVELS - local_levels):
         total = total + from_partner(total, "row", bit)
-    factor = jnp.swapaxes(jnp.linalg.cholesky(total[None]), 1, 2)
+    stacked = jnp.concatenate(
+        [
+            jnp.concatenate([shifted, rows_part], axis=1),
+            jnp.concatenate([total, jnp.zeros_like(rows_part[0])], axis=0)[None],
+        ],
+        axis=0,
+    )
+    factored = cholesky_rows(stacked)
+    leaf_basis = factored[:leaves, SK:, :]
+    factor = jnp.swapaxes(factored[leaves:, :SK, :], 1, 2)
     return (leaf_basis, factor)
 
 

time: 309 us -> 219 us (0.71); the launches traced: 307 us -> 222 us
  other arithmetic: 101 us -> 1.93 us
  Pallas kernels: 19.6 us -> 44.4 us
  waiting for transfers between devices: 162 us -> 150 us
    another operation x10 -> x0, other arithmetic: 98.9 us -> none  [the longest x4 47.1 us: on_device(): lower = jnp.linalg.cholesky(shifted)]
    pallas_call x0 -> x1, Pallas kernels: none -> 16.1 us  [cholesky_rows(): pl.pallas_call(cholesky_kernel, out_shape=jax.ShapeDtypeStruct(stacked.sh...]
    psum x1, waiting for transfers between devices: 107 us -> 93.4 us  [on_device(): samples = lax.psum(samples, 'col')]
    pallas_call x1, Pallas kernels: 19.6 us -> 28.3 us  [accumulate(): pl.pallas_call(sketch_kernel, out_shape=jax.ShapeDtypeStruct((leaves, poi...]
  transfers between devices with their start and end apart: 4 -> 4, of which waited for: 3 -> 4; matrix products, arithmetic and copies ran while one was open for 30% -> 1% of each run, Pallas kernels for 0% -> 0%
where the time goes in v1:
time: 219 us; the launch traced here: 222 us
  waiting for transfers between devices  150 us (68%)
  Pallas kernels  44.4 us (20%)
  between operations  14.2 us (6%)
  local copies, waits for them, and re-layouts  7.32 us (3%)
  matrix products  2.3 us (1%)
    psum x1, waiting for transfers between devices, on_device(): samples = lax.psum(samples, 'col')  93.4 us
    all_gather x1, waiting for transfers between devices, on_device(): owned = lax.all_gather(col_points, 'row', axis=1, tiled=True)  52.3 us
    pallas_call x1, Pallas kernels, accumulate(): pl.pallas_call(sketch_kernel, out_shape=jax.ShapeDtypeStruct((leaves, poi...  28.3 us
    pallas_call x1, Pallas kernels, cholesky_rows(): pl.pallas_call(cholesky_kernel, out_shape=jax.ShapeDtypeStruct(stacked.sh...  16.1 us
  transfers between devices with their start and end apart: 4, of which 4 were waited for; matrix products, arithmetic and copies ran while one was open for 1% of the time, Pallas kernels for 0%

profile of v1, /device:TPU:22, one launch (start us, length us, event | category | flops | bytes accessed | tf_op | source)
XLA Modules:
  0.0 221.6 jit_solution(12853242762923723268)
XLA Ops:
  7.2 0.7 all-gather.2.cloned.1.call-update
  8.0 0.8 multiply_bitcast_fusion
  8.8 0.1 select_select_fusion
  8.9 0.1 copy.17
  9.0 0.2 copy.18
  9.2 0.2 copy.16
  9.4 0.1 subtract_convert_fusion
  9.5 0.7 concatenate.16.row_ref
  10.2 52.3 %all-gather.2.cloned.1.call-done = f32[1,512,8,256]{3,2,0,1:T(8,128)} async-done(((f32[1,16,8,256]{3,2,0,1:T(8,128)}), f32[1,512,8,256]{3,2,0,1:T(8,128)}) %all-gather.2.cloned.1.call-update) | async-done | bytes 4194320 | tf_op jit(solution)/shard_map/all_gather | solution.py:130
  62.5 2.2 copy-done
  64.7 28.3 %shard_map.68 = f32[4,256,128]{2,1,0:T(8,128)} custom-call(s32[4,48]{1,0:T(4,128)S(1)} %copy-done.2, s32[4]{0:T(128)S(1)} %bitcast.14, bf16[4,256,96]{2,1,0:T(8,128)(2,1)S(1)} %concatenate.16.row_ref, f32[512,8,256]{2,1,0:T(8,128)S(1)} %bitcast.12, s32[512,256]{1,0:T(8,128)S(1)} %bitcast.13), custom_call_target="tpu_custom_call" | custom-call | tf_op jit(solution)/shard_map/pallas_call | solution.py:80
  93.1 93.4 %all-reduce.3.cloned.1.call-done = f32[4,256,128]{2,1,0:T(8,128)} async-done(((f32[4,256,128]{2,1,0:T(8,128)}), f32[4,256,128]{2,1,0:T(8,128)}) %all-reduce.3.cloned.1.call-update) | async-done | bytes 524304 | tf_op jit(solution)/shard_map/psum | solution.py:140
  186.5 2.3 %select_reduce_fusion = (f32[4]{0:T(128)S(1)}, f32[4,128,128]{2,1,0:T(8,128)S(1)}) fusion(pred[128,128]{1,0:T(8,128)(4,1)S(1)} %iota_compare_fusion, f32[4,256,128]{2,1,0:T(8,128)} %all-reduce.3.cloned.1.call-done), kind=kOutput, calls=%fused_computation.3 | convolution fusion | flops 201457664 | bytes 802832 | tf_op jit(solution)/shard_map/bri,brk->bik/dot_general | solution.py:143
  188.8 0.1 fusion.2
  188.9 0.1 collective-permute-start
  189.0 1.2 collective-permute-done
  190.3 1.5 collective-permute-start.1
  191.7 0.8 constant_dynamic-slice_fusion
  192.6 2.2 %collective-permute-done.1 = f32[128,128]{1,0:T(8,128)S(1)} collective-permute-done((f32[128,128]{1,0:T(8,128)S(1)}, f32[128,128]{1,0:T(8,128)S(1)}, u32[]{:S(2)}, u32[]{:S(2)}) %collective-permute-start.1) | collective-permute-done | bytes 65568 | tf_op jit(solution)/shard_map/ppermute | solution.py:21
  194.8 0.8 pad_maximum_fusion.in_ref
  195.6 16.1 %shard_map.69 = f32[5,160,128]{2,1,0:T(8,128)} custom-call(f32[5,160,128]{2,1,0:T(8,128)} %pad_maximum_fusion.in_ref), custom_call_target="tpu_custom_call" | custom-call | tf_op jit(solution)/shard_map/pallas_call | solution.py:121
  211.7 0.8 slice_bitcast_fusion
  212.5 1.5 slice.8
  214.0 0.7 copy.23
  (20 shorter events, 0.2 us)
Async XLA Ops:
  7.2 55.3 %copy-start.3 = (s32[4,1]{0,1:T(1,128)S(1)}, s32[4,1]{0,1:T(1,128)}, u32[]{:S(2)}) copy-start(s32[4,1]{0,1:T(1,128)} %param.9) | copy-start | bytes 52
  7.2 55.3 %copy-start.1 = (s32[1,512,256]{2,1,0:T(8,128)S(1)}, s32[1,512,256]{2,1,0:T(8,128)}, u32[]{:S(2)}) copy-start(s32[1,512,256]{2,1,0:T(8,128)} %param.7) | copy-start | bytes 1572868
  7.2 55.3 %copy-start.2 = (s32[4,48]{1,0:T(4,128)S(1)}, s32[4,48]{1,0:T(4,128)}, u32[]{:S(2)}) copy-start(s32[4,48]{1,0:T(4,128)} %slots_ref.1) | copy-start | bytes 2308
  7.2 55.3 %all-gather.2.cloned.1.call-start = ((), (), s32[]{:S(2)}) async-start(), calls=%async_computation | async-start | bytes 4325376 | tf_op jit(solution)/shard_map/all_gather | solution.py:130
  7.9 178.6 %all-reduce.3.cloned.1.call-start = ((), (), s32[]{:S(2)}) async-start(), calls=%async_computation.1 | async-start | bytes 1048576 | tf_op jit(solution)/shard_map/psum | solution.py:140
  62.5 2.2 copy-start
  188.9 1.3 collective-permute-start
  190.3 4.5 %collective-permute-start.1 = (f32[128,128]{1,0:T(8,128)S(1)}, f32[128,128]{1,0:T(8,128)S(1)}, u32[]{:S(2)}, u32[]{:S(2)}) collective-permute-start(f32[128,128]{1,0:T(8,128)S(1)} %add.26), channel_id=1, source_target_pairs={{0,16},{8,24},{16,0},{24,8},{32,48},{40,56},{48,32},{56,40},{64,80... | collective-permute-start | bytes 196616 | tf_op jit(solution)/shard_map/ppermute | solution.py:21
Sparse Core Ops, SparseCore 0:
  10.6 51.9 all-gather.1
  93.2 93.3 all-reduce.2
